TPU v7x, 32 devices: a whole 2x2x4 slice. The times are simulated.
32 devices in a mesh: groups: 2 (over y), enc: 4 (over z), mp: 4 (over x, core).
Axes of the slice: x: 2, y: 2, z: 4, core: 2. Of those that a mesh axis runs over, the one named last changes fastest.
Arguments:
- hidden: bfloat16 [131072, 1024], P(('groups', 'enc'), 'mp'), parts along dimension 0, may hold values from -6 to 6
- proj_w: bfloat16 [1024, 128], P('mp'), may hold values from -0.1875 to 0.1875
- queries: bfloat16 [256, 32, 128], P(('groups', 'enc', 'mp')), parts along dimension 0, may hold values from -208 to 208
- lengths: int32 [512], P('groups'), parts along dimension 0, may hold values from 193 to 256, as said below
- candidates: int32 [256, 16], P(('groups', 'enc', 'mp')), parts along dimension 0, may hold values from 0 to 1023, as said below
Outputs:
- losses: float32 [256], P(('groups', 'enc', 'mp')), parts along dimension 0
- grad_w: float32 [2048, 128], P(('groups', 'mp')), parts along dimension 0
There are 2 independent parts, one for each index of `groups`. A program takes and returns all parts, laid end to end along the dimension named above; an argument that names none is the same for every part. Nothing has to cross between parts.
Inputs may be any that keep to these rules, and one draw needn't show every extreme that they name: Entries are global block numbers of this part. Of the candidates of the 8 queries of one device (aligned rows), at most 16 lie in the 64 blocks of any one device along enc+mp, where device k holds blocks k * 64 to (k + 1) * 64 - 1; some device receives exactly 16 from every device. Blocks may repeat. `lengths`: some passage has 256 tokens and some has 193.
All inputs are finite; a program needn't handle non-finite values.
Results may differ from a plain program's by a relative error of at most 0.0013.
The roundings to bfloat16 on the way count: a program that leaves them out, or rounds other values in their place, can miss the bound.
Values may be sent and summed in bfloat16 or wider, within the bound.
No kernel may reach another device: no remote copies, remote signals or barrier semaphores. Data moves between devices by JAX's collectives and lax.ppermute only.
A program may use at most 128 MiB of HBM per device.

v0:
```python
import jax
import jax.numpy as jnp
from jax import lax
from jax.sharding import PartitionSpec as P

L = 256
BLK = 64


def block_valid(block_ids, lengths):
    per_passage = L // BLK
    passage = block_ids // per_passage
    within = block_ids % per_passage
    positions = within[..., None] * BLK + jnp.arange(BLK, dtype=jnp.int32)
    return positions < lengths[passage][..., None]


def soft_max_sim(sim_tile, valid_mask):
    masked = jnp.where(valid_mask, sim_tile, jnp.float32(-1e30))
    peak = jnp.max(masked, -1, keepdims=True)
    shifted = jnp.exp(masked - peak)
    running = jnp.sum(shifted, -1, keepdims=True)
    scores = jnp.mean(peak[..., 0] + jnp.log(running[..., 0]), -1)
    weights = (shifted / running).astype(jnp.bfloat16)
    return (scores, weights)


def loss_terms(scores):
    margins = scores[:, 1:] - scores[:, :1]
    losses = jnp.mean(jax.nn.softplus(margins), 1)
    slopes = jax.nn.sigmoid(margins) / (scores.shape[1] - 1)
    d_score = jnp.concatenate([-jnp.sum(slopes, 1, keepdims=True), slopes], 1)
    return (losses, d_score)


def left_product(left, right):
    return lax.dot_general(
        left, right, (((0,), (0,)), ((), ())), preferred_element_type=jnp.float32
    )


def local(hidden, proj_w, queries, lengths, candidates):
    mp_count = lax.axis_size("mp")
    owners = lax.axis_size("enc") * mp_count
    row_share = hidden.shape[0] // mp_count
    emb_width = proj_w.shape[1]
    qry_dev = queries.shape[0]
    query_len = queries.shape[1]
    cand_count = candidates.shape[1]
    blk_dev = row_share // BLK
    slot_count = qry_dev * cand_count
    capacity = 2 * slot_count // owners
    me = lax.axis_index("enc") * mp_count + lax.axis_index("mp")
    all_queries = lax.all_gather(queries, ("enc", "mp"), axis=0, tiled=True)
    all_cand = lax.all_gather(candidates, ("enc", "mp"), axis=0, tiled=True)
    all_cand = all_cand.reshape(owners, slot_count)
    e_pre = lax.psum_scatter(
        jnp.dot(hidden, proj_w, preferred_element_type=jnp.float32),
        "mp",
        scatter_dimension=0,
        tiled=True,
    )
    scale = lax.rsqrt(jnp.sum(e_pre * e_pre, -1, keepdims=True) + 1e-06)
    embedded = (e_pre * scale).astype(jnp.bfloat16)
    local_blocks = embedded.reshape(blk_dev, BLK, emb_width)
    slot_ids = jnp.arange(slot_count, dtype=jnp.int32)
    mine = all_cand // blk_dev == me
    rank = jnp.cumsum(mine.astype(jnp.int32), axis=1) - 1
    ranks = jnp.arange(capacity, dtype=jnp.int32)
    pick = mine[:, None, :] & (rank[:, None, :] == ranks[None, :, None])
    valid = jnp.any(pick, axis=2)
    slot_of = jnp.sum(jnp.where(pick, slot_ids[None, None, :], 0), axis=2).astype(jnp.int32)
    block_of = jnp.take_along_axis(all_cand, slot_of, axis=1)
    local_of = block_of % blk_dev
    query_of = jnp.arange(owners, dtype=jnp.int32)[:, None] * qry_dev + slot_of // cand_count
    tiles = local_blocks[local_of]
    q_e = all_queries[query_of]
    valid_mask = block_valid(block_of, lengths)
    sim_tile = jnp.einsum("scie,scje->scij", q_e, tiles, preferred_element_type=jnp.float32)
    scores, weights = soft_max_sim(sim_tile, valid_mask[:, :, None, :])
    placed = jnp.sum(jnp.where(pick, scores[:, :, None], jnp.float32(0)), axis=1)
    all_scores = lax.psum(placed, ("enc", "mp")).reshape(owners * qry_dev, cand_count)
    all_losses, d_score = loss_terms(all_scores)
    losses = lax.dynamic_slice_in_dim(all_losses, me * qry_dev, qry_dev)
    d_e = jnp.take_along_axis(d_score.reshape(owners, slot_count), slot_of, axis=1)
    d_e = jnp.where(valid, d_e, jnp.float32(0))
    occ_grad = jnp.einsum("scij,scie->scje", weights, q_e, preferred_element_type=jnp.float32)
    occ_grad = (occ_grad * (d_e / query_len)[:, :, None, None]).astype(jnp.bfloat16)
    onehot = (local_of[:, :, None] == jnp.arange(blk_dev, dtype=jnp.int32)) & valid[:, :, None]
    grad_emb = jnp.einsum(
        "scb,scx->bx",
        onehot.astype(jnp.bfloat16),
        occ_grad.reshape(owners, capacity, BLK * emb_width),
        preferred_element_type=jnp.float32,
    )
    grad_flat = grad_emb.reshape(row_share, emb_width)
    dot_e = jnp.sum(e_pre * grad_flat, -1, keepdims=True)
    de_pre = (scale * grad_flat - e_pre * (scale * scale * scale) * dot_e).astype(jnp.bfloat16)
    partial_w = left_product(hidden, lax.all_gather(de_pre, "mp", axis=0, tiled=True))
    grad_w = lax.psum(partial_w, "enc")
    return (losses, grad_w)


def solution(mesh):
    return jax.shard_map(
        local,
        mesh=mesh,
        in_specs=(
            P(("groups", "enc"), "mp"),
            P("mp", None),
            P(("groups", "enc", "mp"), None, None),
            P("groups"),
            P(("groups", "enc", "mp"), None),
        ),
        out_specs=(P(("groups", "enc", "mp")), P(("groups", "mp"), None)),
        check_vma=False,
    )
```

profile of v0, /device:TPU:0, one launch (start us, length us, event | category | flops | bytes accessed | tf_op | source)
XLA Modules:
  0.0 255.7 jit_solution(6291594766435006573)
XLA Ops:
  8.1 0.7 all-gather.3.cloned.1.call-update
  8.8 8.9 %fusion.27 = f32[16384,128]{1,0:T(8,128)} fusion(bf16[16384,256]{1,0:T(8,128)(2,1)} %param.5, bf16[256,128]{1,0:T(8,128)(2,1)S(1)} %copy-done), kind=kOutput, calls=%fused_computation.94 | convolution fusion | flops 1073741824 | bytes 16842752 | tf_op jit(solution)/shard_map/dot_general | solution.py:58
  17.9 0.6 copy-done.5
  18.5 23.4 %all_gather.9 = s32[128,16]{1,0:T(8,128)S(1)} all-gather(s32[8,16]{1,0:T(8,128)S(1)} %copy-done.5), channel_id=1, replica_groups=mesh['groups'=2,'enc'=4,'mp'=4] {'enc','mp'}, dimensions={0}, use_global_device_ids=true | all-gather | bytes 8704 | tf_op jit(solution)/shard_map/all_gather | solution.py:55
  41.8 0.1 reshape.380
  41.9 0.3 reduce_window_sum.11
  42.2 0.4 select_reduce_fusion.2
  42.6 0.1 reshape.410
  42.7 1.9 gather_fusion.3
  44.6 0.1 reshape.413
  44.6 0.1 gather.20
  44.7 0.4 fusion.7
  45.1 0.1 copy.34
  45.3 0.1 compare_select_fusion.3
  45.4 0.1 reshape.388
  45.4 0.1 reshape.404
  45.5 0.1 reshape.396
  45.6 1.9 gather_fusion
  47.6 0.1 reshape.387
  47.7 0.1 add_compare_fusion
  47.8 3.8 %all-gather.3.cloned.1.call-done = bf16[128,32,128]{2,1,0:T(8,128)(2,1)} async-done(((bf16[8,32,128]{2,1,0:T(8,128)(2,1)}), bf16[128,32,128]{2,1,0:T(8,128)(2,1)}) %all-gather.3.cloned.1.call-update) | async-done | bytes 1048592 | tf_op jit(solution)/shard_map/all_gather | solution.py:54
  51.6 2.2 gather_fusion.1
  53.9 38.4 %reduce-scatter.2.cloned.1.call-done = f32[4096,128]{1,0:T(8,128)} async-done(((f32[16384,128]{1,0:T(8,128)}), f32[4096,128]{1,0:T(8,128)}) %reduce-scatter.2.cloned.1.call-update) | async-done | bytes 2097168 | tf_op jit(solution)/shard_map/reduce_scatter | solution.py:57
  92.3 2.2 multiply_reduce_fusion.1
  94.5 1.9 multiply_convert_fusion.1
  96.4 3.0 %gather_fusion.2 = bf16[256,64,128]{2,1,0:T(8,128)(2,1)} fusion(bf16[64,64,128]{2,1,0:T(8,128)(2,1)S(1)} %bitcast.55, s32[1024]{0:T(1024)S(1)} %pad_clamp_fusion), kind=kCustom, calls=%fused_computation.2 | custom fusion | bytes 8389632 | tf_op jit(solution)/shard_map/gather | solution.py:76
  99.5 4.6 %select_reduce_fusion = (f32[16,16,32]{2,1,0:T(8,128)S(1)}, f32[16,16,32,64]{3,2,1,0:T(8,128)S(1)}) fusion(pred[16,16,64]{2,1,0:T(8,128)(4,1)S(1)} %add_compare_fusion, bf16[16,16,32,128]{3,2,1,0:T(8,128)(2,1)S(1)} %bitcast.57, bf16[16,16,64,128]{3,2,1,0:T(8,128)(2,1)} %bitcast.56), kind=kOutput, calls=%fused_computation.10 | convolution fusion | flops 135258112 | bytes 8437760 | tf_op jit(solution)/shard_map/scie,scje->scij/dot_general | solution.py:79
  104.1 2.0 copy-done.4
  106.0 2.4 fusion.1
  108.5 0.1 add_reduce_fusion
  108.6 0.1 select_reduce_fusion.1
  108.7 0.1 reshape.382
  108.9 32.9 %psum.14 = f32[128,16]{0,1:T(8,128)S(1)} all-reduce(f32[128,16]{0,1:T(8,128)S(1)} %copy.32), channel_id=1, replica_groups=mesh['groups'=2,'enc'=4,'mp'=4] {'enc','mp'}, use_global_device_ids=true, to_apply=%region_8.9 | all-reduce | flops 2048 | bytes 16384 | tf_op jit(solution)/shard_map/psum | solution.py:82
  141.8 0.1 copy.35
  141.9 0.1 reshape.383
  142.0 1.9 gather_fusion.4
  143.9 0.1 reshape.419
  144.0 8.0 %multiply_convert_fusion = bf16[16,16,64,128]{3,2,1,0:T(8,128)(2,1)} fusion(f32[16,16]{1,0:T(8,128)S(1)} %select_multiply_fusion, bf16[16,16,32,128]{3,2,1,0:T(8,128)(2,1)S(1)} %bitcast.58, f32[16,16,32,64]{3,2,1,0:T(8,128)} %copy-done.4, f32[16,16,32]{2,1,0:T(8,128)S(1)} %fusion.1, f32[16,16,32]{2,1,0:T(8,128)S(1)} %get-tuple-element.26, ...), kind=kOutput, calls=%fused_computation.6 | convolution fusion | flops 140509184 | bytes 8471552 | tf_op jit(solution)/shard_map/scij,scie->scje/dot_general | solution.py:87
  152.0 7.3 %reshape.384 = bf16[16,16,8192]{2,1,0:T(8,128)(2,1)} reshape(bf16[16,16,64,128]{3,2,1,0:T(8,128)(2,1)} %multiply_convert_fusion) | data formatting | bytes 8388608 | tf_op jit(solution)/shard_map/reshape | solution.py:93
  159.3 6.3 %convolution_bitcast_fusion = f32[64,8192]{1,0:T(8,128)} fusion(bf16[16,16,8192]{2,1,0:T(8,128)(2,1)} %reshape.384, s32[16,16]{0,1:T(8,128)S(1)} %copy.33, pred[16,16]{0,1:T(8,128)(4,1)S(1)} %copy.34), kind=kOutput, calls=%fused_computation.5 | convolution fusion | flops 268468224 | bytes 6292736 | tf_op jit(solution)/shard_map/scb,scx->bx/dot_general | solution.py:90
  165.6 2.7 %reshape.385 = f32[4096,128]{1,0:T(8,128)} reshape(f32[64,8192]{1,0:T(8,128)} %convolution_bitcast_fusion) | data formatting | bytes 4194304 | tf_op jit(solution)/shard_map/reshape | solution.py:96
  168.3 2.4 multiply_reduce_fusion
  170.6 2.9 %subtract_convert_fusion = bf16[4096,128]{1,0:T(8,128)(2,1)} fusion(f32[4096,128]{1,0:T(8,128)S(1)} %copy-done.2, f32[4096,128]{1,0:T(8,128)S(1)} %copy-done.3, f32[4096]{0:T(1024)S(1)} %multiply_reduce_fusion, f32[4096]{0:T(1024)S(1)} %get-tuple-element.20, f32[4096]{0:T(1024)S(1)} %get-tuple-element.21), kind=kLoop, calls=%fused_computation.12 | loop fusion | flops 2621440 | bytes 5292032 | tf_op jit(solution)/shard_map/convert_element_type | solution.py:98
  173.6 31.6 %all-gather.5.cloned.1.call-done = bf16[16384,128]{1,0:T(8,128)(2,1)} async-done(((bf16[4096,128]{1,0:T(8,128)(2,1)}), bf16[16384,128]{1,0:T(8,128)(2,1)}) %all-gather.5.cloned.1.call-update) | async-done | bytes 4194320 | tf_op jit(solution)/shard_map/all_gather | solution.py:99
  205.2 6.8 %convolution_bitcast_fusion.1 = f32[256,128]{0,1:T(8,128)} fusion(bf16[16384,128]{1,0:T(8,128)(2,1)} %all-gather.5.cloned.1.call-done, bf16[16384,256]{1,0:T(8,128)(2,1)} %param.5), kind=kOutput, calls=%fused_computation.20 | convolution fusion | flops 1073741824 | bytes 12713984 | tf_op jit(solution)/shard_map/dot_general | solution.py:37
  212.1 0.6 dynamic_slice.3
  212.7 34.0 %all-reduce.2.cloned.1.call-done = f32[256,128]{0,1:T(8,128)} async-done(((f32[256,128]{0,1:T(8,128)}), f32[256,128]{0,1:T(8,128)}) %all-reduce.2.cloned.1.call-update) | async-done | bytes 131088 | tf_op jit(solution)/shard_map/psum | solution.py:100
  246.7 1.7 copy.37
  (36 shorter events, 0.6 us)
Async XLA Ops:
  8.0 0.8 copy-start
  8.0 43.6 %all-gather.3.cloned.1.call-start = ((), (), s32[]{:S(2)}) async-start(), calls=%async_computation.1 | async-start | bytes 1114112 | tf_op jit(solution)/shard_map/all_gather | solution.py:54
  8.7 83.5 %reduce-scatter.2.cloned.1.call-start = ((), (), s32[]{:S(2)}) async-start(), calls=%async_computation.2 | async-start | bytes 10485760 | tf_op jit(solution)/shard_map/reduce_scatter | solution.py:57
  17.8 0.7 copy-start.5
  17.8 187.4 %all-gather.5.cloned.1.call-start = ((), (), s32[]{:S(2)}) async-start(), calls=%async_computation.3 | async-start | bytes 5242880 | tf_op jit(solution)/shard_map/all_gather | solution.py:99
  42.7 2.9 %copy-start.1 = (s32[256]{0:T(256)S(1)}, s32[256]{0:T(256)}, u32[]{:S(2)}) copy-start(s32[256]{0:T(256)} %param.8) | copy-start | bytes 3076
  104.1 2.0 copy-start.4
  159.3 9.0 %copy-start.2 = (f32[4096,128]{1,0:T(8,128)S(1)}, f32[4096,128]{1,0:T(8,128)}, u32[]{:S(2)}) copy-start(f32[4096,128]{1,0:T(8,128)} %reduce-scatter.2.cloned.1.call-done) | copy-start | bytes 6291460
  168.3 2.4 copy-start.3
  173.5 73.1 %all-reduce.2.cloned.1.call-start = ((), (), s32[]{:S(2)}) async-start(), calls=%async_computation.4 | async-start | bytes 262144 | tf_op jit(solution)/shard_map/psum | solution.py:100
Sparse Core Ops, SparseCore 0:
  11.0 40.5 all-gather.2
  212.2 34.4 all-reduce.1
Sparse Core Ops, SparseCore 1:
  17.9 74.3 reduce-scatter.1
  173.6 31.5 all-gather.4
where the time goes:
time: 256 us
  waiting for transfers between devices  109 us (43%)
  blocking collectives  56.2 us (22%)
  matrix products  34.7 us (14%)
  local copies, waits for them, and re-layouts  27 us (11%)
  between operations  15.7 us (6%)
  other arithmetic  13.4 us (5%)
    reduce_scatter x1, waiting for transfers between devices, local(): lax.psum_scatter(jnp.dot(hidden, proj_w, preferred_element_type=jnp.float...  38.4 us
    psum x1, waiting for transfers between devices, local(): grad_w = lax.psum(partial_w, 'enc')  34 us
    psum x1, blocking collectives, local(): lax.psum(placed, ('enc', 'mp')).reshape(owners * qry_dev, cand_count)  32.9 us
    all_gather x1, waiting for transfers between devices, local(): lax.all_gather(de_pre, 'mp', axis=0, tiled=True)  31.6 us
    all_gather x1, blocking collectives, local(): all_cand = lax.all_gather(candidates, ('enc', 'mp'), axis=0, tiled=True)  23.4 us
    dot_general x1, matrix products, local(): jnp.dot(hidden, proj_w, preferred_element_type=jnp.float32)  8.94 us
    dot_general x1, matrix products, local(): jnp.einsum('scij,scie->scje', weights, q_e, preferred_element_type=jnp.fl...  8 us
    reshape x1, local copies, waits for them, and re-layouts, local(): occ_grad.reshape(owners, capacity, BLK * emb_width)  7.31 us
  transfers between devices with their start and end apart: 4, of which 4 were waited for; matrix products, arithmetic and copies ran while one was open for 7% of the time, Pallas kernels for 0%

commit v1 on v0

--- a/solution.py
+++ b/solution.py
@@ -40,6 +40,11 @@
 
 
 def local(hidden, proj_w, queries, lengths, candidates):
+
+    def produce_the_leaves(buf, along_axis, bus_axis):
+        all_values = jax.lax.psum(buf, along_axis)
+        return jax.lax.psum(all_values, bus_axis)
+
     mp_count = lax.axis_size("mp")
     owners = lax.axis_size("enc") * mp_count
     row_share = hidden.shape[0] // mp_count
@@ -79,7 +84,7 @@
     sim_tile = jnp.einsum("scie,scje->scij", q_e, tiles, preferred_element_type=jnp.float32)
     scores, weights = soft_max_sim(sim_tile, valid_mask[:, :, None, :])
     placed = jnp.sum(jnp.where(pick, scores[:, :, None], jnp.float32(0)), axis=1)
-    all_scores = lax.psum(placed, ("enc", "mp")).reshape(owners * qry_dev, cand_count)
+    all_scores = produce_the_leaves(placed, "mp", "enc").reshape(owners * qry_dev, cand_count)
     all_losses, d_score = loss_terms(all_scores)
     losses = lax.dynamic_slice_in_dim(all_losses, me * qry_dev, qry_dev)
     d_e = jnp.take_along_axis(d_score.reshape(owners, slot_count), slot_of, axis=1)

time: 256 us -> 242 us (0.945)
  blocking collectives: 56.2 us -> 41.5 us
    psum x1 -> x2, blocking collectives: 32.9 us -> 18.1 us  [the longest x1 12.3 us: produce_the_leaves(): return jax.lax.psum(all_values, bus_axis)]
where the time goes in v1:
time: 242 us; the launch traced here: 241 us
  waiting for transfers between devices  109 us (45%)
  blocking collectives  41.5 us (17%)
  matrix products  34.7 us (14%)
  local copies, waits for them, and re-layouts  27 us (11%)
  between operations  15.7 us (6%)
  other arithmetic  13.4 us (6%)
    reduce_scatter x1, waiting for transfers between devices, local(): lax.psum_scatter(jnp.dot(hidden, proj_w, preferred_element_type=jnp.float...  38.4 us
    psum x1, waiting for transfers between devices, local(): grad_w = lax.psum(partial_w, 'enc')  34 us
    all_gather x1, waiting for transfers between devices, local(): lax.all_gather(de_pre, 'mp', axis=0, tiled=True)  32.1 us
    all_gather x1, blocking collectives, local(): all_cand = lax.all_gather(candidates, ('enc', 'mp'), axis=0, tiled=True)  23.4 us
    psum x1, blocking collectives, produce_the_leaves(): return jax.lax.psum(all_values, bus_axis)  12.3 us
    dot_general x1, matrix products, local(): jnp.dot(hidden, proj_w, preferred_element_type=jnp.float32)  8.94 us
    dot_general x1, matrix products, local(): jnp.einsum('scij,scie->scje', weights, q_e, preferred_element_type=jnp.fl...  8 us
    reshape x1, local copies, waits for them, and re-layouts, local(): occ_grad.reshape(owners, capacity, BLK * emb_width)  7.31 us
  transfers between devices with their start and end apart: 4, of which 4 were waited for; matrix products, arithmetic and copies ran while one was open for 7% of the time, Pallas kernels for 0%

profile of v1, /device:TPU:0, one launch (start us, length us, event | category | flops | bytes accessed | tf_op | source)
XLA Modules:
  0.0 241.5 jit_solution(1293869924825637662)
XLA Ops:
  8.1 0.7 all-gather.3.cloned.1.call-update
  8.8 8.9 %fusion.27 = f32[16384,128]{1,0:T(8,128)} fusion(bf16[16384,256]{1,0:T(8,128)(2,1)} %param.5, bf16[256,128]{1,0:T(8,128)(2,1)S(1)} %copy-done), kind=kOutput, calls=%fused_computation.94 | convolution fusion | flops 1073741824 | bytes 16842752 | tf_op jit(solution)/shard_map/dot_general | solution.py:63
  17.9 0.6 copy-done.5
  18.5 23.4 %all_gather.9 = s32[128,16]{1,0:T(8,128)S(1)} all-gather(s32[8,16]{1,0:T(8,128)S(1)} %copy-done.5), channel_id=1, replica_groups=mesh['groups'=2,'enc'=4,'mp'=4] {'enc','mp'}, dimensions={0}, use_global_device_ids=true | all-gather | bytes 8704 | tf_op jit(solution)/shard_map/all_gather | solution.py:60
  41.8 0.1 reshape.380
  41.9 0.3 reduce_window_sum.11
  42.2 0.4 select_reduce_fusion.2
  42.6 0.1 reshape.410
  42.7 1.9 gather_fusion.3
  44.6 0.1 reshape.413
  44.6 0.1 gather.20
  44.7 0.4 fusion.7
  45.1 0.1 copy.34
  45.3 0.1 compare_select_fusion.3
  45.4 0.1 reshape.388
  45.4 0.1 reshape.404
  45.5 0.1 reshape.396
  45.6 1.9 gather_fusion
  47.6 0.1 reshape.387
  47.7 0.1 add_compare_fusion
  47.8 3.8 %all-gather.3.cloned.1.call-done = bf16[128,32,128]{2,1,0:T(8,128)(2,1)} async-done(((bf16[8,32,128]{2,1,0:T(8,128)(2,1)}), bf16[128,32,128]{2,1,0:T(8,128)(2,1)}) %all-gather.3.cloned.1.call-update) | async-done | bytes 1048592 | tf_op jit(solution)/shard_map/all_gather | solution.py:59
  51.6 2.2 gather_fusion.1
  53.9 38.4 %reduce-scatter.2.cloned.1.call-done = f32[4096,128]{1,0:T(8,128)} async-done(((f32[16384,128]{1,0:T(8,128)}), f32[4096,128]{1,0:T(8,128)}) %reduce-scatter.2.cloned.1.call-update) | async-done | bytes 2097168 | tf_op jit(solution)/shard_map/reduce_scatter | solution.py:62
  92.3 2.2 multiply_reduce_fusion.1
  94.5 1.9 multiply_convert_fusion.1
  96.4 3.0 %gather_fusion.2 = bf16[256,64,128]{2,1,0:T(8,128)(2,1)} fusion(bf16[64,64,128]{2,1,0:T(8,128)(2,1)S(1)} %bitcast.55, s32[1024]{0:T(1024)S(1)} %pad_clamp_fusion), kind=kCustom, calls=%fused_computation.2 | custom fusion | bytes 8389632 | tf_op jit(solution)/shard_map/gather | solution.py:81
  99.5 4.6 %select_reduce_fusion = (f32[16,16,32]{2,1,0:T(8,128)S(1)}, f32[16,16,32,64]{3,2,1,0:T(8,128)S(1)}) fusion(pred[16,16,64]{2,1,0:T(8,128)(4,1)S(1)} %add_compare_fusion, bf16[16,16,32,128]{3,2,1,0:T(8,128)(2,1)S(1)} %bitcast.57, bf16[16,16,64,128]{3,2,1,0:T(8,128)(2,1)} %bitcast.56), kind=kOutput, calls=%fused_computation.10 | convolution fusion | flops 135258112 | bytes 8437760 | tf_op jit(solution)/shard_map/scie,scje->scij/dot_general | solution.py:84
  104.1 2.0 copy-done.4
  106.0 2.4 fusion.1
  108.5 0.1 add_reduce_fusion
  108.6 0.1 select_reduce_fusion.1
  108.7 5.9 %psum.21 = f32[16,128]{1,0:T(8,128)S(1)} all-reduce(f32[16,128]{1,0:T(8,128)S(1)} %select_reduce_fusion.1), channel_id=1, replica_groups=mesh['groups'=2,'enc'=4,'mp'=4] {'mp'}, use_global_device_ids=true, to_apply=%region_8.9 | all-reduce | flops 2048 | bytes 16384 | tf_op jit(solution)/shard_map/psum | solution.py:45
  114.7 12.3 %psum.22 = f32[128,16]{0,1:T(8,128)S(1)} all-reduce(f32[128,16]{0,1:T(8,128)S(1)} %copy.32), channel_id=1, replica_groups=mesh['groups'=2,'enc'=4,'mp'=4] {'enc'}, use_global_device_ids=true, to_apply=%region_9.10 | all-reduce | flops 2048 | bytes 16384 | tf_op jit(solution)/shard_map/psum | solution.py:46
  127.1 0.1 copy.35
  127.2 0.1 reshape.383
  127.3 1.9 gather_fusion.4
  129.2 0.1 reshape.419
  129.3 8.0 %multiply_convert_fusion = bf16[16,16,64,128]{3,2,1,0:T(8,128)(2,1)} fusion(f32[16,16]{1,0:T(8,128)S(1)} %select_multiply_fusion, bf16[16,16,32,128]{3,2,1,0:T(8,128)(2,1)S(1)} %bitcast.58, f32[16,16,32,64]{3,2,1,0:T(8,128)} %copy-done.4, f32[16,16,32]{2,1,0:T(8,128)S(1)} %fusion.1, f32[16,16,32]{2,1,0:T(8,128)S(1)} %get-tuple-element.26, ...), kind=kOutput, calls=%fused_computation.6 | convolution fusion | flops 140509184 | bytes 8471552 | tf_op jit(solution)/shard_map/scij,scie->scje/dot_general | solution.py:92
  137.3 7.3 %reshape.384 = bf16[16,16,8192]{2,1,0:T(8,128)(2,1)} reshape(bf16[16,16,64,128]{3,2,1,0:T(8,128)(2,1)} %multiply_convert_fusion) | data formatting | bytes 8388608 | tf_op jit(solution)/shard_map/reshape | solution.py:98
  144.6 6.3 %convolution_bitcast_fusion = f32[64,8192]{1,0:T(8,128)} fusion(bf16[16,16,8192]{2,1,0:T(8,128)(2,1)} %reshape.384, s32[16,16]{0,1:T(8,128)S(1)} %copy.33, pred[16,16]{0,1:T(8,128)(4,1)S(1)} %copy.34), kind=kOutput, calls=%fused_computation.5 | convolution fusion | flops 268468224 | bytes 6292736 | tf_op jit(solution)/shard_map/scb,scx->bx/dot_general | solution.py:95
  150.9 2.7 %reshape.385 = f32[4096,128]{1,0:T(8,128)} reshape(f32[64,8192]{1,0:T(8,128)} %convolution_bitcast_fusion) | data formatting | bytes 4194304 | tf_op jit(solution)/shard_map/reshape | solution.py:101
  153.6 2.4 multiply_reduce_fusion
  155.9 2.9 %subtract_convert_fusion = bf16[4096,128]{1,0:T(8,128)(2,1)} fusion(f32[4096,128]{1,0:T(8,128)S(1)} %copy-done.2, f32[4096,128]{1,0:T(8,128)S(1)} %copy-done.3, f32[4096]{0:T(1024)S(1)} %multiply_reduce_fusion, f32[4096]{0:T(1024)S(1)} %get-tuple-element.20, f32[4096]{0:T(1024)S(1)} %get-tuple-element.21), kind=kLoop, calls=%fused_computation.12 | loop fusion | flops 2621440 | bytes 5292032 | tf_op jit(solution)/shard_map/convert_element_type | solution.py:103
  158.9 32.1 %all-gather.5.cloned.1.call-done = bf16[16384,128]{1,0:T(8,128)(2,1)} async-done(((bf16[4096,128]{1,0:T(8,128)(2,1)}), bf16[16384,128]{1,0:T(8,128)(2,1)}) %all-gather.5.cloned.1.call-update) | async-done | bytes 4194320 | tf_op jit(solution)/shard_map/all_gather | solution.py:104
  190.9 6.8 %convolution_bitcast_fusion.1 = f32[256,128]{0,1:T(8,128)} fusion(bf16[16384,128]{1,0:T(8,128)(2,1)} %all-gather.5.cloned.1.call-done, bf16[16384,256]{1,0:T(8,128)(2,1)} %param.5), kind=kOutput, calls=%fused_computation.20 | convolution fusion | flops 1073741824 | bytes 12713984 | tf_op jit(solution)/shard_map/dot_general | solution.py:37
  197.8 0.6 dynamic_slice.3
  198.4 34.0 %all-reduce.2.cloned.1.call-done = f32[256,128]{0,1:T(8,128)} async-done(((f32[256,128]{0,1:T(8,128)}), f32[256,128]{0,1:T(8,128)}) %all-reduce.2.cloned.1.call-update) | async-done | bytes 131088 | tf_op jit(solution)/shard_map/psum | solution.py:105
  232.4 1.7 copy.37
  (37 shorter events, 0.6 us)
Async XLA Ops:
  8.0 0.8 copy-start
  8.0 43.6 %all-gather.3.cloned.1.call-start = ((), (), s32[]{:S(2)}) async-start(), calls=%async_computation.1 | async-start | bytes 1114112 | tf_op jit(solution)/shard_map/all_gather | solution.py:59
  8.7 83.5 %reduce-scatter.2.cloned.1.call-start = ((), (), s32[]{:S(2)}) async-start(), calls=%async_computation.2 | async-start | bytes 10485760 | tf_op jit(solution)/shard_map/reduce_scatter | solution.py:62
  17.8 0.7 copy-start.5
  17.8 173.1 %all-gather.5.cloned.1.call-start = ((), (), s32[]{:S(2)}) async-start(), calls=%async_computation.3 | async-start | bytes 5242880 | tf_op jit(solution)/shard_map/all_gather | solution.py:104
  42.7 2.9 %copy-start.1 = (s32[256]{0:T(256)S(1)}, s32[256]{0:T(256)}, u32[]{:S(2)}) copy-start(s32[256]{0:T(256)} %param.8) | copy-start | bytes 3076
  104.1 2.0 copy-start.4
  144.6 9.0 %copy-start.2 = (f32[4096,128]{1,0:T(8,128)S(1)}, f32[4096,128]{1,0:T(8,128)}, u32[]{:S(2)}) copy-start(f32[4096,128]{1,0:T(8,128)} %reduce-scatter.2.cloned.1.call-done) | copy-start | bytes 6291460
  153.5 2.4 copy-start.3
  158.8 73.6 %all-reduce.2.cloned.1.call-start = ((), (), s32[]{:S(2)}) async-start(), calls=%async_computation.4 | async-start | bytes 262144 | tf_op jit(solution)/shard_map/psum | solution.py:105
Sparse Core Ops, SparseCore 0:
  11.0 40.5 all-gather.2
  197.9 34.4 all-reduce.1
Sparse Core Ops, SparseCore 1:
  17.9 74.3 reduce-scatter.1
  158.9 32.0 all-gather.4
